TPU v7x, 32 devices: a whole 2x2x4 slice. The times are simulated.
32 devices in a mesh: feat: 8 (over y, x, core), tok: 4 (over z).
Axes of the slice: x: 2, y: 2, z: 4, core: 2. Of those that a mesh axis runs over, the one named last changes fastest.
Arguments:
- residual: bfloat16 [256, 4608], P('tok', 'feat'), may hold values from -700 to 700
- enc_weight: bfloat16 [4608, 8192], P(None, ('feat', 'tok')), may hold values from -0.09375 to 0.09375
- enc_bias: float32 [8192], P(('feat', 'tok')), may hold values from -3 to 3
- threshold: float32 [8192], P(('feat', 'tok')), may hold values from 0.25 to 2.5
- probe_weight: bfloat16 [8192, 16], P(('feat', 'tok')), may hold values from -0.375 to 0.375
- probe_bias: float32 [16], replicated, may hold values from -3 to 3
- labels: int32 [256], replicated, may hold values from 0 to 15
Outputs:
- probe_grad: float32 [8192, 16], P(('feat', 'tok'))
- token_loss: float32 [256], P(('feat', 'tok'))
All inputs are finite; a program needn't handle non-finite values.
Results may differ from a plain program's by a relative error of at most 0.0034.
Values may be sent and summed in bfloat16 or wider, within the bound.
No kernel may reach another device: no remote copies, remote signals or barrier semaphores. Data moves between devices by JAX's collectives and lax.ppermute only.
A program may use at most 64 MiB of HBM per device.

v0:
```python
import jax
import jax.numpy as jnp
from jax import lax
from jax.sharding import PartitionSpec as P

epsilon = 1e-06
smooth_width = 0.125


def normalize(values, squares):
    full_width = values.shape[1] * lax.axis_size("feat")
    row_scale = lax.rsqrt(squares / full_width + epsilon)
    return (values * row_scale[:, None]).astype(jnp.bfloat16)


def local(residual, enc_weight, enc_bias, threshold, probe_weight, probe_bias, labels):
    values = residual.astype(jnp.float32)
    squares = lax.psum(jnp.sum(values * values, axis=1), "feat")
    normed = normalize(values, squares)
    all_tokens = lax.all_gather(normed, "tok", axis=0, tiled=True)
    preact = jnp.dot(
        lax.all_gather(all_tokens, "feat", axis=1, tiled=True),
        enc_weight,
        preferred_element_type=jnp.float32,
    )
    encode_preact = preact
    encode_preact = encode_preact + enc_bias
    features = (encode_preact * jax.nn.sigmoid((encode_preact - threshold) / smooth_width)).astype(
        jnp.bfloat16
    )
    partial_value = jnp.dot(features, probe_weight, preferred_element_type=jnp.float32)
    num_tokens = features.shape[0]
    share_rows = num_tokens // lax.axis_size(("feat", "tok"))
    position = lax.axis_index(("feat", "tok"))
    class_ids = jnp.arange(probe_weight.shape[1], dtype=jnp.int32)
    logits = lax.psum(partial_value, ("feat", "tok"))
    softmax_logits = logits
    softmax_logits = softmax_logits + probe_bias
    exps = jnp.exp(softmax_logits)
    totals = jnp.sum(exps, axis=1, keepdims=True)
    onehot = (labels[:, None] == class_ids[None, :]).astype(jnp.float32)
    losses = jnp.log(totals[:, 0]) - jnp.sum(onehot * softmax_logits, axis=1)
    losses, delta = (losses, (exps / totals - onehot).astype(jnp.bfloat16))
    token_loss = lax.dynamic_slice_in_dim(losses, position * share_rows, share_rows, 0)
    gradient = jnp.dot(features.T, delta, preferred_element_type=jnp.float32)
    return (gradient, token_loss)


def solution(mesh):
    in_specs = (
        P("tok", "feat"),
        P(None, ("feat", "tok")),
        P(("feat", "tok")),
        P(("feat", "tok")),
        P(("feat", "tok"), None),
        P(),
        P(),
    )
    out_specs = (P(("feat", "tok"), None), P(("feat", "tok")))
    return jax.shard_map(local, mesh=mesh, in_specs=in_specs, out_specs=out_specs, check_vma=False)
```

profile of v0, /device:TPU:0, one launch (start us, length us, event | category | flops | bytes accessed | tf_op | source)
XLA Modules:
  0.0 118.5 jit_solution(7145613870447156144)
XLA Ops:
  7.2 0.0 copy-start
  7.2 0.0 all-gather.2.cloned.1.call-start
  7.2 1.2 fusion
  8.4 15.2 %psum.14 = f32[64]{0:T(128)S(1)} all-reduce(f32[64]{0:T(128)S(1)} %fusion), channel_id=1, replica_groups=mesh['feat'=8,'tok'=4] {'feat'}, use_global_device_ids=true, to_apply=%region_1.0 | all-reduce | flops 64 | bytes 512 | tf_op jit(solution)/shard_map/psum | solution.py:18
  23.5 1.0 fusion.1
  24.5 14.9 %all_gather.6 = bf16[256,576]{1,0:T(8,128)(2,1)S(1)} all-gather(bf16[64,576]{1,0:T(8,128)(2,1)S(1)} %fusion.1), channel_id=1, replica_groups=mesh['feat'=8,'tok'=4] {'tok'}, dimensions={0}, use_global_device_ids=true | all-gather | bytes 368640 | tf_op jit(solution)/shard_map/all_gather | solution.py:20
  39.4 0.9 copy.10
  40.3 0.0 all-gather.2.cloned.1.call-update
  40.3 0.0 copy-start.1
  40.3 0.0 copy-start.2
  40.4 0.0 copy-start.3
  40.4 27.8 %all-gather.2.cloned.1.call-done = bf16[256,4608]{0,1:T(8,128)(2,1)} async-done(((bf16[256,576]{0,1:T(8,128)(2,1)}), bf16[256,4608]{0,1:T(8,128)(2,1)}) %all-gather.2.cloned.1.call-update) | async-done | bytes 2359312 | tf_op jit(solution)/shard_map/all_gather | solution.py:22
  68.1 0.0 copy-done
  68.1 2.5 %multiply_convert_fusion = bf16[256,256]{1,0:T(8,128)(2,1)S(1)} fusion(bf16[256,4608]{0,1:T(8,128)(2,1)} %all-gather.2.cloned.1.call-done, bf16[4608,256]{1,0:T(8,128)(2,1)S(1)} %copy-done, f32[256]{0:T(256)} %param.10, f32[256]{0:T(256)} %param.9), kind=kOutput, calls=%fused_computation.1 | convolution fusion | flops 604504064 | bytes 4851712 | tf_op jit(solution)/shard_map/dot_general | solution.py:21
  70.7 0.0 copy-done.1
  70.7 0.1 fusion.6
  70.8 39.3 %psum.15 = f32[256,16]{0,1:T(8,128)S(1)} all-reduce(f32[256,16]{0,1:T(8,128)S(1)} %fusion.6), channel_id=1, replica_groups=mesh['feat'=8,'tok'=4] {'feat','tok'}, use_global_device_ids=true, to_apply=%region_2.0 | all-reduce | flops 4096 | bytes 32768 | tf_op jit(solution)/shard_map/psum | solution.py:36
  110.2 0.0 copy-done.2
  110.2 0.0 copy-done.3
  110.2 0.1 select_reduce_fusion
  110.3 0.8 fusion.2
  111.1 0.6 dynamic_slice.3
  (2 shorter events, 0.0 us)
Async XLA Ops:
  7.2 61.0 %copy-start = (bf16[4608,256]{1,0:T(8,128)(2,1)S(1)}, bf16[4608,256]{1,0:T(8,128)(2,1)}, u32[]{:S(2)}) copy-start(bf16[4608,256]{1,0:T(8,128)(2,1)} %param.8) | copy-start | bytes 7077892
  7.2 60.9 %all-gather.2.cloned.1.call-start = ((), (), s32[]{:S(2)}) async-start(), calls=%async_computation | async-start | bytes 2654208 | tf_op jit(solution)/shard_map/all_gather | solution.py:22
  40.3 30.3 %copy-start.1 = (bf16[256,16]{0,1:T(8,128)(2,1)S(1)}, bf16[256,16]{0,1:T(8,128)(2,1)}, u32[]{:S(2)}) copy-start(bf16[256,16]{0,1:T(8,128)(2,1)} %param.11) | copy-start | bytes 24580
  40.3 69.8 %copy-start.2 = (s32[256]{0:T(256)S(1)}, s32[256]{0:T(256)}, u32[]{:S(2)}) copy-start(s32[256]{0:T(256)} %param.13) | copy-start | bytes 3076
  40.4 69.8 %copy-start.3 = (f32[16]{0:T(128)S(1)}, f32[16]{0:T(128)}, u32[]{:S(2)}) copy-start(f32[16]{0:T(128)} %param.12) | copy-start | bytes 196
Sparse Core Ops, SparseCore 0:
  40.5 27.6 all-gather.1
where the time goes:
time: 119 us
  blocking collectives  69.4 us (58%)
  waiting for transfers between devices  27.8 us (23%)
  between operations  14.1 us (12%)
  matrix products  3.49 us (3%)
  other arithmetic  2.24 us (2%)
  local copies, waits for them, and re-layouts  1.5 us (1%)
    psum x1, blocking collectives, local(): logits = lax.psum(partial_value, ('feat', 'tok'))  39.3 us
    all_gather x1, waiting for transfers between devices, local(): lax.all_gather(all_tokens, 'feat', axis=1, tiled=True)  27.8 us
    psum x1, blocking collectives, local(): squares = lax.psum(jnp.sum(values * values, axis=1), 'feat')  15.2 us
    all_gather x1, blocking collectives, local(): all_tokens = lax.all_gather(normed, 'tok', axis=0, tiled=True)  14.9 us
    dot_general x1, matrix products, local(): jnp.dot(lax.all_gather(all_tokens, 'feat', axis=1, tiled=True), enc_weigh...  2.53 us
  transfers between devices with their start and end apart: 1, of which 1 were waited for; matrix products, arithmetic and copies ran while one was open for 0% of the time, Pallas kernels for 0%

commit v1 on v0

--- a/solution.py
+++ b/solution.py
@@ -33,7 +33,7 @@
     share_rows = num_tokens // lax.axis_size(("feat", "tok"))
     position = lax.axis_index(("feat", "tok"))
     class_ids = jnp.arange(probe_weight.shape[1], dtype=jnp.int32)
-    logits = lax.psum(partial_value, ("feat", "tok"))
+    logits = jnp.sum(lax.all_gather(partial_value, ("feat", "tok")), axis=0)
     softmax_logits = logits
     softmax_logits = softmax_logits + probe_bias
     exps = jnp.exp(softmax_logits)

time: 119 us -> 151 us (1.27)
  blocking collectives: 69.4 us -> 102 us
    all_gather x0 -> x1, blocking collectives: none -> 71.6 us  [local(): logits = jnp.sum(lax.all_gather(partial_value, ('feat', 'tok')), axis=0)]
    psum x1 -> x0, blocking collectives: 39.3 us -> none  [local(): logits = lax.psum(partial_value, ('feat', 'tok'))]
where the time goes in v1:
time: 151 us
  blocking collectives  102 us (68%)
  waiting for transfers between devices  27.8 us (18%)
  between operations  14.1 us (9%)
  matrix products  3.48 us (2%)
  other arithmetic  2.29 us (2%)
  local copies, waits for them, and re-layouts  1.66 us (1%)
    all_gather x1, blocking collectives, local(): logits = jnp.sum(lax.all_gather(partial_value, ('feat', 'tok')), axis=0)  71.6 us
    all_gather x1, waiting for transfers between devices, local(): lax.all_gather(all_tokens, 'feat', axis=1, tiled=True)  27.8 us
    psum x1, blocking collectives, local(): squares = lax.psum(jnp.sum(values * values, axis=1), 'feat')  15.2 us
    all_gather x1, blocking collectives, local(): all_tokens = lax.all_gather(normed, 'tok', axis=0, tiled=True)  14.9 us
  transfers between devices with their start and end apart: 1, of which 1 were waited for; matrix products, arithmetic and copies ran while one was open for 0% of the time, Pallas kernels for 0%

profile of v1, /device:TPU:0, one launch (start us, length us, event | category | flops | bytes accessed | tf_op | source)
XLA Modules:
  0.0 151.0 jit_solution(14659095292995916565)
XLA Ops:
  7.2 0.0 copy-start
  7.2 0.0 all-gather.3.cloned.1.call-start
  7.2 1.2 fusion
  8.4 15.2 %psum.7 = f32[64]{0:T(128)S(1)} all-reduce(f32[64]{0:T(128)S(1)} %fusion), channel_id=1, replica_groups=mesh['feat'=8,'tok'=4] {'feat'}, use_global_device_ids=true, to_apply=%region_1.0 | all-reduce | flops 64 | bytes 512 | tf_op jit(solution)/shard_map/psum | solution.py:18
  23.5 1.0 fusion.1
  24.5 14.9 %all_gather.12 = bf16[256,576]{1,0:T(8,128)(2,1)S(1)} all-gather(bf16[64,576]{1,0:T(8,128)(2,1)S(1)} %fusion.1), channel_id=1, replica_groups=mesh['feat'=8,'tok'=4] {'tok'}, dimensions={0}, use_global_device_ids=true | all-gather | bytes 368640 | tf_op jit(solution)/shard_map/all_gather | solution.py:20
  39.4 0.9 copy.10
  40.3 0.0 all-gather.3.cloned.1.call-update
  40.3 0.0 copy-start.1
  40.3 0.0 copy-start.2
  40.4 0.0 copy-start.3
  40.4 27.8 %all-gather.3.cloned.1.call-done = bf16[256,4608]{0,1:T(8,128)(2,1)} async-done(((bf16[256,576]{0,1:T(8,128)(2,1)}), bf16[256,4608]{0,1:T(8,128)(2,1)}) %all-gather.3.cloned.1.call-update) | async-done | bytes 2359312 | tf_op jit(solution)/shard_map/all_gather | solution.py:22
  68.1 0.0 copy-done
  68.1 2.5 %multiply_convert_fusion = bf16[256,256]{1,0:T(8,128)(2,1)S(1)} fusion(bf16[256,4608]{0,1:T(8,128)(2,1)} %all-gather.3.cloned.1.call-done, bf16[4608,256]{1,0:T(8,128)(2,1)S(1)} %copy-done, f32[256]{0:T(256)} %param.10, f32[256]{0:T(256)} %param.9), kind=kOutput, calls=%fused_computation.2 | convolution fusion | flops 604504064 | bytes 4851712 | tf_op jit(solution)/shard_map/dot_general | solution.py:21
  70.7 0.0 copy-done.1
  70.7 0.1 fusion.6
  70.8 71.6 %all-gather = f32[8192,16]{0,1:T(8,128)S(1)} all-gather(f32[256,16]{0,1:T(8,128)S(1)} %fusion.6), channel_id=2, replica_groups=mesh['feat'=8,'tok'=4] {'feat','tok'}, dimensions={0}, use_global_device_ids=true | all-gather | bytes 540672 | tf_op jit(solution)/shard_map/all_gather | solution.py:36
  142.4 0.2 copy.11
  142.6 0.1 bitcast_reduce_fusion
  142.6 0.0 copy-done.2
  142.6 0.0 copy-done.3
  142.6 0.1 select_reduce_fusion
  142.7 0.8 fusion.2
  143.6 0.6 dynamic_slice.3
  (2 shorter events, 0.0 us)
Async XLA Ops:
  7.2 61.0 %copy-start = (bf16[4608,256]{1,0:T(8,128)(2,1)S(1)}, bf16[4608,256]{1,0:T(8,128)(2,1)}, u32[]{:S(2)}) copy-start(bf16[4608,256]{1,0:T(8,128)(2,1)} %param.8) | copy-start | bytes 7077892
  7.2 60.9 %all-gather.3.cloned.1.call-start = ((), (), s32[]{:S(2)}) async-start(), calls=%async_computation | async-start | bytes 2654208 | tf_op jit(solution)/shard_map/all_gather | solution.py:22
  40.3 30.3 %copy-start.1 = (bf16[256,16]{0,1:T(8,128)(2,1)S(1)}, bf16[256,16]{0,1:T(8,128)(2,1)}, u32[]{:S(2)}) copy-start(bf16[256,16]{0,1:T(8,128)(2,1)} %param.11) | copy-start | bytes 24580
  40.3 102.3 %copy-start.2 = (s32[256]{0:T(256)S(1)}, s32[256]{0:T(256)}, u32[]{:S(2)}) copy-start(s32[256]{0:T(256)} %param.13) | copy-start | bytes 3076
  40.4 102.3 %copy-start.3 = (f32[16]{0:T(128)S(1)}, f32[16]{0:T(128)}, u32[]{:S(2)}) copy-start(f32[16]{0:T(128)} %param.12) | copy-start | bytes 196
Sparse Core Ops, SparseCore 0:
  40.5 27.6 all-gather.2
